TPU v7x, 512 devices: a whole 4x8x8 slice. The times are simulated.
512 devices in a mesh: row: 64 (over y, x, core), col: 8 (over z).
Axes of the slice: x: 4, y: 8, z: 8, core: 2. Of those that a mesh axis runs over, the one named last changes fastest.
Arguments:
- panel_cols: float32 [16384, 256], P('row'), may hold values from -60 to 60, as said below
- affinity: float32 [16384, 16384], P('row', 'col'), may hold values from -8 to 8, as said below
Outputs:
- updated: float32 [16384, 16384], P('row', 'col')
- band_block: float32 [256, 256], replicated
Inputs may be any that keep to these rules, and one draw needn't show every extreme that they name: affinity holds a symmetric matrix in the stored column order of the steps. panel_cols has full column rank.
All inputs are finite; a program needn't handle non-finite values.
Results may differ from a plain program's by a relative error of at most 0.000071.
Values sent between devices are 32-bit elements; how exact they have to be, the bound alone decides.
No kernel may reach another device: no remote copies, remote signals or barrier semaphores. Data moves between devices by JAX's collectives and lax.ppermute only.
A program may use at most 64 MiB of HBM per device.

v0:
```python
import jax
import jax.numpy as jnp
from jax import lax
from jax.sharding import PartitionSpec as P


def shards(panel_cols, affinity):
    high = lax.Precision.HIGHEST
    local_rows = panel_cols.shape[0]
    piece_rows = local_rows // lax.axis_size("col")
    col_place = lax.axis_index("col")
    gram_sum = lax.psum(jnp.dot(panel_cols.T, panel_cols, precision=high), "row")
    lower_factor = jnp.linalg.cholesky(gram_sum)
    ortho_basis = jax.scipy.linalg.solve_triangular(lower_factor, panel_cols.T, lower=True).T
    own_basis = lax.dynamic_slice_in_dim(ortho_basis, col_place * piece_rows, piece_rows, 0)
    arrived = lax.all_gather(own_basis, "row", axis=0, tiled=True)
    partial_sum = jnp.dot(affinity, arrived, precision=high)
    partial_sum, basis_cols = (partial_sum, arrived)
    moment = lax.psum(partial_sum, "col")
    band_block = lax.psum(jnp.dot(ortho_basis.T, moment, precision=high), "row")
    corrected = moment - 0.5 * jnp.dot(ortho_basis, band_block, precision=high)
    own_corrected = lax.dynamic_slice_in_dim(corrected, col_place * piece_rows, piece_rows, 0)
    update_cols = lax.all_gather(own_corrected, "row", axis=0, tiled=True)
    updated = affinity - jnp.dot(ortho_basis, update_cols.T, precision=high)
    updated = updated - jnp.dot(corrected, basis_cols.T, precision=high)
    return (updated, band_block)


def solution(mesh):
    placed = (P("row", None), P("row", "col"))
    return jax.shard_map(
        shards, mesh=mesh, in_specs=placed, out_specs=(P("row", "col"), P()), check_vma=False
    )
```

profile of v0, /device:TPU:1, one launch (start us, length us, event | category | flops | bytes accessed | tf_op | source)
XLA Modules:
  0.0 722.9 jit_solution(2886932835697183772)
XLA Ops:
  7.2 2.3 fusion.16
  9.6 196.8 %all-reduce.5.cloned.1.call-done = f32[256,256]{0,1:T(8,128)} async-done(((f32[256,256]{0,1:T(8,128)}), f32[256,256]{0,1:T(8,128)}) %all-reduce.5.cloned.1.call-update) | async-done | bytes 262160 | tf_op jit(solution)/shard_map/psum | solution.py:12
  206.4 1.1 copy.8
  207.5 1.0 fusion.1
  208.5 11.7 %cholesky.50 = f32[128,128]{1,0:T(8,128)S(1)} custom-call(f32[128,128]{1,0:T(8,128)S(1)} %cholesky.118), custom_call_target="Cholesky" | custom-call | tf_op jit(solution)/shard_map/jit(cholesky)/cholesky | solution.py:13
  220.3 9.8 %custom-call.15 = f32[1,128,128]{1,2,0:T(8,128)S(1)} custom-call(f32[1,128,128]{2,1,0:T(8,128)S(1)} %get-tuple-element.23), custom_call_target="InvertDiagBlocksLowerTriangular" | custom-call | tf_op jit(solution)/shard_map/jit(cholesky)/cholesky | solution.py:13
  230.1 0.2 constant_dynamic-update-slice_fusion
  230.3 0.3 convolution_subtract_fusion.3
  230.6 11.7 %cholesky.105 = f32[128,128]{1,0:T(8,128)S(1)} custom-call(f32[128,128]{1,0:T(8,128)S(1)} %convolution_subtract_fusion.3), custom_call_target="Cholesky" | custom-call | tf_op jit(solution)/shard_map/jit(cholesky)/cholesky | solution.py:13
  242.3 0.7 compare_reduce_fusion
  244.4 4.1 while.1
  244.5 0.6 fusion.31
  245.1 1.4 bitcast_dynamic-update-slice_fusion.2
  246.5 0.6 fusion.31
  247.1 1.4 bitcast_dynamic-update-slice_fusion.2
  248.5 19.7 %custom-call.16 = f32[2,128,128]{1,2,0:T(8,128)S(1)} custom-call(f32[2,128,128]{2,1,0:T(8,128)S(1)} %get-tuple-element.9), custom_call_target="InvertDiagBlocksLowerTriangular" | custom-call | tf_op jit(solution)/shard_map/jit(_solve_triangular)/triangular_solve | solution.py:14
  268.1 0.3 fusion.5
  268.5 0.4 convolution_subtract_fusion.2
  268.9 0.3 fusion.8
  269.2 0.1 fusion.4
  269.3 0.7 copy.9
  270.1 80.7 %all-gather.3.cloned.1.call-done = f32[2048,256]{1,0:T(8,128)} async-done(((f32[32,256]{1,0:T(8,128)}), f32[2048,256]{1,0:T(8,128)}) %all-gather.3.cloned.1.call-update) | async-done | bytes 2097168 | tf_op jit(solution)/shard_map/all_gather | solution.py:16
  350.7 4.2 convolution_bitcast_fusion
  355.0 71.6 %all-reduce.7.cloned.1.call-done = f32[256,256]{1,0:T(8,128)} async-done(((f32[256,256]{1,0:T(8,128)}), f32[256,256]{1,0:T(8,128)}) %all-reduce.7.cloned.1.call-update) | async-done | bytes 262160 | tf_op jit(solution)/shard_map/psum | solution.py:19
  426.6 2.0 fusion.2
  428.7 193.9 %all-reduce.9.cloned.1.call-done = f32[256,256]{1,0:T(8,128)} async-done(((f32[256,256]{1,0:T(8,128)}), f32[256,256]{1,0:T(8,128)}) %all-reduce.9.cloned.1.call-update) | async-done | bytes 262160 | tf_op jit(solution)/shard_map/psum | solution.py:20
  622.6 1.6 fusion
  624.2 0.6 constant_dynamic-slice_fusion.1
  624.9 82.1 %all-gather.5.cloned.1.call-done = f32[2048,256]{1,0:T(8,128)} async-done(((f32[32,256]{1,0:T(8,128)}), f32[2048,256]{1,0:T(8,128)}) %all-gather.5.cloned.1.call-update) | async-done | bytes 2097168 | tf_op jit(solution)/shard_map/all_gather | solution.py:23
  707.0 5.3 convolution_subtract_fusion.1
  712.3 3.4 convolution_subtract_fusion
  715.6 0.7 copy.26
  (28 shorter events, 0.5 us)
Async XLA Ops:
  7.2 199.3 %all-reduce.5.cloned.1.call-start = ((), (), s32[]{:S(2)}) async-start(), calls=%async_computation | async-start | bytes 524288 | tf_op jit(solution)/shard_map/psum | solution.py:12
  9.5 258.6 %copy-start.2 = (f32[256,256]{1,0:T(8,128)S(1)}, f32[256,256]{1,0:T(8,128)}, u32[]{:S(2)}) copy-start(f32[256,256]{1,0:T(8,128)} %param.2) | copy-start | bytes 786436
  9.6 341.1 %all-gather.3.cloned.1.call-start = ((), (), s32[]{:S(2)}) async-start(), calls=%async_computation.1 | async-start | bytes 2129920 | tf_op jit(solution)/shard_map/all_gather | solution.py:16
  220.2 130.5 %copy-start = (f32[256,2048]{1,0:T(8,128)S(1)}, f32[256,2048]{1,0:T(8,128)}, u32[]{:S(2)}) copy-start(f32[256,2048]{1,0:T(8,128)} %param.3) | copy-start | bytes 6291460
  270.0 156.6 %all-reduce.7.cloned.1.call-start = ((), (), s32[]{:S(2)}) async-start(), calls=%async_computation.2 | async-start | bytes 524288 | tf_op jit(solution)/shard_map/psum | solution.py:19
  355.0 267.6 %all-reduce.9.cloned.1.call-start = ((), (), s32[]{:S(2)}) async-start(), calls=%async_computation.3 | async-start | bytes 524288 | tf_op jit(solution)/shard_map/psum | solution.py:20
  428.7 278.3 %all-gather.5.cloned.1.call-start = ((), (), s32[]{:S(2)}) async-start(), calls=%async_computation.4 | async-start | bytes 2129920 | tf_op jit(solution)/shard_map/all_gather | solution.py:23
  707.0 5.3 copy-start.1
  712.2 3.4 copy-start.3
Sparse Core Ops, SparseCore 0:
  12.0 194.3 all-reduce.4
  270.1 80.5 all-gather.2
  355.1 71.4 all-reduce.6
  430.5 192.0 all-reduce.8
  626.4 80.5 all-gather.4
where the time goes:
time: 723 us
  waiting for transfers between devices  625 us (86%)
  other arithmetic  54.8 us (8%)
  matrix products  20.3 us (3%)
  between operations  15.2 us (2%)
    psum x1, waiting for transfers between devices, shards(): lax.psum(jnp.dot(panel_cols.T, panel_cols, precision=high), 'row')  197 us
    psum x1, waiting for transfers between devices, shards(): band_block = lax.psum(jnp.dot(ortho_basis.T, moment, precision=high), 'row')  194 us
    all_gather x1, waiting for transfers between devices, shards(): update_cols = lax.all_gather(own_corrected, 'row', axis=0, tiled=True)  82.1 us
    all_gather x1, waiting for transfers between devices, shards(): arrived = lax.all_gather(own_basis, 'row', axis=0, tiled=True)  80.7 us
    psum x1, waiting for transfers between devices, shards(): moment = lax.psum(partial_sum, 'col')  71.6 us
    another operation x6, other arithmetic, shards(): lower_factor = jnp.linalg.cholesky(gram_sum)  34 us
    another operation x3, other arithmetic, shards(): jax.scipy.linalg.solve_triangular(lower_factor, panel_cols.T, lower=True)  19.7 us
  transfers between devices with their start and end apart: 5, of which 5 were waited for; matrix products, arithmetic and copies ran while one was open for 0% of the time, Pallas kernels for 0%

commit v1 on v0

--- a/solution.py
+++ b/solution.py
@@ -16,7 +16,10 @@
     arrived = lax.all_gather(own_basis, "row", axis=0, tiled=True)
     partial_sum = jnp.dot(affinity, arrived, precision=high)
     partial_sum, basis_cols = (partial_sum, arrived)
-    moment = lax.psum(partial_sum, "col")
+    num = lax.psum(1, "col")
+    moment = partial_sum
+    for idx in [[(k0, k0 ^ q) for k0 in range(num)] for q in (1, 2, 4, 8, 16) if q < num]:
+        moment = moment + lax.ppermute(moment, axis_name="col", perm=idx)
     band_block = lax.psum(jnp.dot(ortho_basis.T, moment, precision=high), "row")
     corrected = moment - 0.5 * jnp.dot(ortho_basis, band_block, precision=high)
     own_corrected = lax.dynamic_slice_in_dim(corrected, col_place * piece_rows, piece_rows, 0)

time: 723 us -> 685 us (0.947)
  waiting for transfers between devices: 625 us -> 573 us
  starting transfers between devices: 0.21 us -> 16.5 us
    psum x1 -> x0, waiting for transfers between devices: 71.6 us -> none  [shards(): moment = lax.psum(partial_sum, 'col')]
    ppermute x0 -> x3, waiting for transfers between devices: none -> 29.1 us  [shards(): moment = moment + lax.ppermute(moment, axis_name='col', perm=idx)]
    ppermute x0 -> x3, starting transfers between devices: none -> 16.2 us  [shards(): moment = moment + lax.ppermute(moment, axis_name='col', perm=idx)]
    psum x1, waiting for transfers between devices: 194 us -> 184 us  [shards(): band_block = lax.psum(jnp.dot(ortho_basis.T, moment, precision=high), 'row')]
  transfers between devices with their start and end apart: 5 -> 7, of which waited for: 5 -> 7; matrix products, arithmetic and copies ran while one was open for 0% -> 0% of each run, Pallas kernels for 0% -> 0%
where the time goes in v1:
time: 685 us
  waiting for transfers between devices  573 us (84%)
  other arithmetic  54.8 us (8%)
  matrix products  18.6 us (3%)
  starting transfers between devices  16.5 us (2%)
  between operations  15.2 us (2%)
  local copies, waits for them, and re-layouts  6.99 us (1%)
    psum x1, waiting for transfers between devices, shards(): lax.psum(jnp.dot(panel_cols.T, panel_cols, precision=high), 'row')  197 us
    psum x1, waiting for transfers between devices, shards(): band_block = lax.psum(jnp.dot(ortho_basis.T, moment, precision=high), 'row')  184 us
    all_gather x1, waiting for transfers between devices, shards(): update_cols = lax.all_gather(own_corrected, 'row', axis=0, tiled=True)  82.2 us
    all_gather x1, waiting for transfers between devices, shards(): arrived = lax.all_gather(own_basis, 'row', axis=0, tiled=True)  80.7 us
    another operation x6, other arithmetic, shards(): lower_factor = jnp.linalg.cholesky(gram_sum)  33.9 us
    ppermute x3, waiting for transfers between devices, shards(): moment = moment + lax.ppermute(moment, axis_name='col', perm=idx)  29.1 us
    another operation x3, other arithmetic, shards(): jax.scipy.linalg.solve_triangular(lower_factor, panel_cols.T, lower=True)  19.7 us
    ppermute x3, starting transfers between devices, shards(): moment = moment + lax.ppermute(moment, axis_name='col', perm=idx)  16.2 us
  transfers between devices with their start and end apart: 7, of which 7 were waited for; matrix products, arithmetic and copies ran while one was open for 0% of the time, Pallas kernels for 0%

profile of v1, /device:TPU:1, one launch (start us, length us, event | category | flops | bytes accessed | tf_op | source)
XLA Modules:
  0.0 685.1 jit_solution(11867380836916276557)
XLA Ops:
  7.2 2.3 fusion.16
  9.6 196.8 %all-reduce.4.cloned.1.call-done = f32[256,256]{0,1:T(8,128)} async-done(((f32[256,256]{0,1:T(8,128)}), f32[256,256]{0,1:T(8,128)}) %all-reduce.4.cloned.1.call-update) | async-done | bytes 262160 | tf_op jit(solution)/shard_map/psum | solution.py:12
  206.4 1.1 copy.7
  207.5 1.0 fusion.1
  208.5 11.7 %cholesky.50 = f32[128,128]{1,0:T(8,128)S(1)} custom-call(f32[128,128]{1,0:T(8,128)S(1)} %cholesky.118), custom_call_target="Cholesky" | custom-call | tf_op jit(solution)/shard_map/jit(cholesky)/cholesky | solution.py:13
  220.3 9.8 %custom-call.15 = f32[1,128,128]{1,2,0:T(8,128)S(1)} custom-call(f32[1,128,128]{2,1,0:T(8,128)S(1)} %get-tuple-element.23), custom_call_target="InvertDiagBlocksLowerTriangular" | custom-call | tf_op jit(solution)/shard_map/jit(cholesky)/cholesky | solution.py:13
  230.6 11.7 %cholesky.105 = f32[128,128]{1,0:T(8,128)S(1)} custom-call(f32[128,128]{1,0:T(8,128)S(1)} %convolution_subtract_fusion.3), custom_call_target="Cholesky" | custom-call | tf_op jit(solution)/shard_map/jit(cholesky)/cholesky | solution.py:13
  242.3 0.6 compare_reduce_fusion
  244.3 4.0 while.1
  244.5 0.6 fusion.31
  245.0 1.3 bitcast_dynamic-update-slice_fusion.2
  246.4 0.6 fusion.31
  247.0 1.3 bitcast_dynamic-update-slice_fusion.2
  248.3 19.7 %custom-call.16 = f32[2,128,128]{1,2,0:T(8,128)S(1)} custom-call(f32[2,128,128]{2,1,0:T(8,128)S(1)} %get-tuple-element.9), custom_call_target="InvertDiagBlocksLowerTriangular" | custom-call | tf_op jit(solution)/shard_map/jit(_solve_triangular)/triangular_solve | solution.py:14
  268.3 0.4 convolution_subtract_fusion.2
  269.1 0.7 copy.8
  269.9 80.7 %all-gather.3.cloned.1.call-done = f32[2048,256]{1,0:T(8,128)} async-done(((f32[32,256]{1,0:T(8,128)}), f32[2048,256]{1,0:T(8,128)}) %all-gather.3.cloned.1.call-update) | async-done | bytes 2097168 | tf_op jit(solution)/shard_map/all_gather | solution.py:16
  350.5 3.5 convolution_bitcast_fusion
  354.1 3.3 collective-permute-start
  357.3 6.2 collective-permute-done
  363.6 4.3 collective-permute-start.1
  367.9 11.3 %collective-permute-done.1 = f32[256,256]{1,0:T(8,128)S(1)} collective-permute-done((f32[256,256]{1,0:T(8,128)S(1)}, f32[256,256]{1,0:T(8,128)S(1)}, u32[]{:S(2)}, u32[]{:S(2)}) %collective-permute-start.1) | collective-permute-done | bytes 262176 | tf_op jit(solution)/shard_map/ppermute | solution.py:22
  379.3 8.5 %collective-permute-start.2 = (f32[256,256]{1,0:T(8,128)S(1)}, f32[256,256]{1,0:T(8,128)S(1)}, u32[]{:S(2)}, u32[]{:S(2)}) collective-permute-start(f32[256,256]{1,0:T(8,128)S(1)} %add.43), channel_id=1, source_target_pairs={{0,4},{1,5},{2,6},{3,7},{4,0},{5,1},{6,2},{7,3},{8,12},{9,13},{10,... | collective-permute-start | bytes 786440 | tf_op jit(solution)/shard_map/ppermute | solution.py:22
  387.8 11.6 %collective-permute-done.2 = f32[256,256]{1,0:T(8,128)S(1)} collective-permute-done((f32[256,256]{1,0:T(8,128)S(1)}, f32[256,256]{1,0:T(8,128)S(1)}, u32[]{:S(2)}, u32[]{:S(2)}) %collective-permute-start.2) | collective-permute-done | bytes 262176 | tf_op jit(solution)/shard_map/ppermute | solution.py:22
  399.4 1.1 fusion.2
  400.8 184.0 %all-reduce.6.cloned.1.call-done = f32[256,256]{1,0:T(8,128)} async-done(((f32[256,256]{1,0:T(8,128)}), f32[256,256]{1,0:T(8,128)}) %all-reduce.6.cloned.1.call-update) | async-done | bytes 262160 | tf_op jit(solution)/shard_map/psum | solution.py:23
  584.8 1.5 fusion
  586.4 0.6 constant_dynamic-slice_fusion.1
  587.0 82.2 %all-gather.5.cloned.1.call-done = f32[2048,256]{1,0:T(8,128)} async-done(((f32[32,256]{1,0:T(8,128)}), f32[2048,256]{1,0:T(8,128)}) %all-gather.5.cloned.1.call-update) | async-done | bytes 2097168 | tf_op jit(solution)/shard_map/all_gather | solution.py:26
  669.2 5.3 convolution_subtract_fusion.1
  674.5 3.4 convolution_subtract_fusion
  677.8 0.7 copy.22
  (34 shorter events, 2.0 us)
Async XLA Ops:
  7.2 199.3 %all-reduce.4.cloned.1.call-start = ((), (), s32[]{:S(2)}) async-start(), calls=%async_computation | async-start | bytes 524288 | tf_op jit(solution)/shard_map/psum | solution.py:12
  9.5 258.4 %copy-start.2 = (f32[256,256]{1,0:T(8,128)S(1)}, f32[256,256]{1,0:T(8,128)}, u32[]{:S(2)}) copy-start(f32[256,256]{1,0:T(8,128)} %param.2) | copy-start | bytes 786436
  9.6 340.9 %all-gather.3.cloned.1.call-start = ((), (), s32[]{:S(2)}) async-start(), calls=%async_computation.1 | async-start | bytes 2129920 | tf_op jit(solution)/shard_map/all_gather | solution.py:16
  220.2 130.3 %copy-start = (f32[256,2048]{1,0:T(8,128)S(1)}, f32[256,2048]{1,0:T(8,128)}, u32[]{:S(2)}) copy-start(f32[256,2048]{1,0:T(8,128)} %param.3) | copy-start | bytes 6291460
  269.8 315.0 %all-reduce.6.cloned.1.call-start = ((), (), s32[]{:S(2)}) async-start(), calls=%async_computation.2 | async-start | bytes 524288 | tf_op jit(solution)/shard_map/psum | solution.py:23
  354.1 9.5 %collective-permute-start = (f32[256,256]{1,0:T(8,128)S(1)}, f32[256,256]{1,0:T(8,128)S(1)}, u32[]{:S(2)}, u32[]{:S(2)}) collective-permute-start(f32[256,256]{1,0:T(8,128)S(1)} %convolution_bitcast_fusion), channel_id=1, source_target_pairs={{0,1},{1,0},{2,3},{3,2},{4,5},{5,4},{6,7},{7,6},{8,9},{9,8},{10,11... | collective-permute-start | bytes 786440 | tf_op jit(solution)/shard_map/ppermute | solution.py:22
  363.6 15.6 %collective-permute-start.1 = (f32[256,256]{1,0:T(8,128)S(1)}, f32[256,256]{1,0:T(8,128)S(1)}, u32[]{:S(2)}, u32[]{:S(2)}) collective-permute-start(f32[256,256]{1,0:T(8,128)S(1)} %add.42), channel_id=1, source_target_pairs={{0,2},{1,3},{2,0},{3,1},{4,6},{5,7},{6,4},{7,5},{8,10},{9,11},{10,... | collective-permute-start | bytes 786440 | tf_op jit(solution)/shard_map/ppermute | solution.py:22
  379.3 20.1 %collective-permute-start.2 = (f32[256,256]{1,0:T(8,128)S(1)}, f32[256,256]{1,0:T(8,128)S(1)}, u32[]{:S(2)}, u32[]{:S(2)}) collective-permute-start(f32[256,256]{1,0:T(8,128)S(1)} %add.43), channel_id=1, source_target_pairs={{0,4},{1,5},{2,6},{3,7},{4,0},{5,1},{6,2},{7,3},{8,12},{9,13},{10,... | collective-permute-start | bytes 786440 | tf_op jit(solution)/shard_map/ppermute | solution.py:22
  400.6 268.6 %all-gather.5.cloned.1.call-start = ((), (), s32[]{:S(2)}) async-start(), calls=%async_computation.3 | async-start | bytes 2129920 | tf_op jit(solution)/shard_map/all_gather | solution.py:26
  669.2 5.3 copy-start.1
  674.5 3.4 copy-start.3
Sparse Core Ops, SparseCore 0:
  12.0 194.3 all-reduce.3
  269.9 80.5 all-gather.2
  400.7 184.1 all-reduce.5
  588.6 80.5 all-gather.4
